TPU v7x, 32 devices: a whole 2x2x4 slice. The times are simulated.
32 devices in a mesh: groups: 2 (over y), frame: 4 (over x, core), row: 4 (over z).
Axes of the slice: x: 2, y: 2, z: 4, core: 2. Of those that a mesh axis runs over, the one named last changes fastest.
Arguments:
- query_in: bfloat16 [8, 4, 64, 2240], P(('groups', 'frame'), 'row'), parts along dimension 0, may hold values from -6 to 6
- key_in: bfloat16 [8, 4, 64, 2240], P(('groups', 'frame'), 'row'), parts along dimension 0, may hold values from -216 to 216
- value_in: bfloat16 [8, 4, 64, 2240], P(('groups', 'frame'), 'row'), parts along dimension 0, may hold values from -6 to 6
- stream_in: bfloat16 [8, 4, 64, 2240], P(('groups', 'frame'), 'row'), parts along dimension 0, may hold values from -6 to 6
- attn_gain: bfloat16 [2240], replicated, may hold values from 0.5 to 1.5
- ffn_gain: bfloat16 [2240], replicated, may hold values from 0.5 to 1.5
- in_weight: bfloat16 [2240, 2, 3360], P('row', None, 'frame'), may hold values from -0.125 to 0.125
- conv_weight: bfloat16 [9, 2, 3360], P(None, None, 'frame'), may hold values from -3.5 to 3.5
- out_weight: bfloat16 [3360, 2240], P('frame'), may hold values from -0.109375 to 0.109375
Outputs:
- stream_out: bfloat16 [8, 4, 64, 2240], P(('groups', 'frame'), 'row'), parts along dimension 0
- block_out: bfloat16 [8, 4, 64, 2240], P(('groups', 'frame'), 'row'), parts along dimension 0
There are 2 independent parts, one for each index of `groups`. A program takes and returns all parts, laid end to end along the dimension named above; an argument that names none is the same for every part. Nothing has to cross between parts.
All inputs are finite; a program needn't handle non-finite values.
Results may differ from a plain program's by a relative error of at most 0.01.
Values may be sent and summed in bfloat16 or wider, within the bound.
No kernel may reach another device: no remote copies, remote signals or barrier semaphores. Data moves between devices by JAX's collectives and lax.ppermute only.
A program may use at most 64 MiB of HBM per device.

v0:
```python
import jax
import jax.numpy as jnp
from jax import lax
from jax.sharding import PartitionSpec as P

HEADS = 20
HEAD_DIM = 112
NORM_EPS = 1e-06
SHARE_EPS = 1e-06


def padded_2(cells, sides, width):
    for axis, dim in sides:
        count = lax.axis_size(axis)
        ends = count - 1
        head = lax.slice_in_dim(cells, 0, width, axis=dim)
        tail = lax.slice_in_dim(cells, cells.shape[dim] - width, cells.shape[dim], axis=dim)
        cells = jnp.concatenate(
            [
                lax.ppermute(tail, axis, [(i, (i + 1) % count) for i in range(ends)]),
                cells,
                lax.ppermute(head, axis, [((i + 1) % count, i) for i in range(ends)]),
            ],
            axis=dim,
        )
    return cells


def rms_norm(features):
    return features * lax.rsqrt(jnp.mean(features * features, axis=-1, keepdims=True) + NORM_EPS)


def depthwise(padded, conv_taps, row_count, col_count, half_width):
    widened = jnp.pad(padded, ((0, 0), (0, 0), (1, 1), (0, 0)))
    summed = jnp.zeros((padded.shape[0], row_count, col_count, padded.shape[3]), jnp.float32)
    for row_off in range(3):
        for col_off in range(3):
            window = widened[
                :, row_off : row_off + row_count, col_off : col_off + col_count, :
            ].astype(jnp.float32)
            summed = summed + window * conv_taps[row_off * 3 + col_off]
    return (summed[..., :half_width] * jax.nn.silu(summed[..., half_width:])).astype(jnp.bfloat16)


def local(
    query_in, key_in, value_in, stream_in, attn_gain, ffn_gain, in_weight, conv_weight, out_weight
):
    frame_count, row_count, col_count, model_width = query_in.shape
    token_count = frame_count * row_count * col_count
    local_gated = in_weight.shape[2]
    highest = lax.Precision.HIGHEST
    key_pos = jnp.maximum(key_in, 0).reshape(token_count, HEADS, HEAD_DIM)
    value_heads = value_in.reshape(token_count, HEADS, HEAD_DIM)
    local_state = jnp.einsum(
        "thi,thj->ihj", key_pos, value_heads, preferred_element_type=jnp.float32
    ).reshape(HEAD_DIM, model_width)
    local_total = jnp.sum(key_pos.reshape(token_count, model_width), axis=0, dtype=jnp.float32)
    state_share, total_share = (
        lax.psum_scatter(
            local_state.astype(jnp.bfloat16), "row", scatter_dimension=1, tiled=True
        ).astype(jnp.float32),
        lax.psum_scatter(
            local_total.astype(jnp.bfloat16), "row", scatter_dimension=0, tiled=True
        ).astype(jnp.float32),
    )
    state_share, total_share = lax.psum((state_share, total_share), "frame")
    kv_state, key_total = (
        lax.all_gather(state_share, "row", axis=1, tiled=True),
        lax.all_gather(total_share, "row", axis=0, tiled=True),
    )
    query_pos = jnp.maximum(query_in, 0).reshape(token_count, HEADS, HEAD_DIM).astype(jnp.float32)
    numerator = jnp.einsum(
        "thi,ihj->thj", query_pos, kv_state.reshape(HEAD_DIM, HEADS, HEAD_DIM), precision=highest
    )
    denominator = jnp.einsum(
        "thi,hi->th", query_pos, key_total.reshape(HEADS, HEAD_DIM), precision=highest
    )
    attended = (numerator / (denominator[:, :, None] + SHARE_EPS)).reshape(token_count, model_width)
    stream_flat = stream_in.reshape(token_count, model_width).astype(jnp.float32)
    stream_out = (stream_flat + attn_gain.astype(jnp.float32) * rms_norm(attended)).astype(
        jnp.bfloat16
    )
    normed = (rms_norm(stream_out.astype(jnp.float32)) * ffn_gain.astype(jnp.float32)).astype(
        jnp.bfloat16
    )
    normed_grid = normed.reshape(frame_count, row_count, col_count, model_width)
    in_full = lax.all_gather(in_weight, "row", axis=0, tiled=True).reshape(
        model_width, 2 * local_gated
    )
    conv_taps = conv_weight.reshape(9, 2 * local_gated).astype(jnp.float32)
    frame_piece = lax.all_gather(normed_grid, "frame", axis=0, tiled=True)
    piece_frames = frame_piece.shape[0]
    piece_rows = frame_piece.shape[1]
    projected = jnp.dot(
        frame_piece.reshape(piece_frames * piece_rows * col_count, model_width),
        in_full,
        preferred_element_type=jnp.float32,
    )
    expanded = (
        jax.nn.silu(projected)
        .astype(jnp.bfloat16)
        .reshape(piece_frames, piece_rows, col_count, 2 * local_gated)
    )
    padded_expanded = padded_2(expanded, (("row", 1),), 1)
    hidden = depthwise(padded_expanded, conv_taps, row_count, col_count, local_gated)
    hidden_flat = hidden.reshape(-1, local_gated)
    ffn_rows = lax.psum_scatter(
        jnp.dot(hidden_flat, out_weight, preferred_element_type=jnp.float32).astype(jnp.bfloat16),
        "frame",
        scatter_dimension=0,
        tiled=True,
    ).astype(jnp.float32)
    block_out = (stream_out.astype(jnp.float32) + ffn_rows).astype(jnp.bfloat16)
    grid_shape = (frame_count, row_count, col_count, model_width)
    return (stream_out.reshape(grid_shape), block_out.reshape(grid_shape))


def solution(mesh):
    in_specs = (
        P(("groups", "frame"), "row", None, None),
        P(("groups", "frame"), "row", None, None),
        P(("groups", "frame"), "row", None, None),
        P(("groups", "frame"), "row", None, None),
        P(),
        P(),
        P("row", None, "frame"),
        P(None, None, "frame"),
        P("frame", None),
    )
    out_specs = (
        P(("groups", "frame"), "row", None, None),
        P(("groups", "frame"), "row", None, None),
    )
    return jax.shard_map(local, mesh=mesh, in_specs=in_specs, out_specs=out_specs, check_vma=False)
```

profile of v0, /device:TPU:0, one launch (start us, length us, event | category | flops | bytes accessed | tf_op | source)
XLA Modules:
  0.0 293.6 jit_solution(11495132540162727477)
XLA Ops:
  7.2 1.1 fusion.21
  8.3 0.4 reshape.204
  8.7 1.4 reshape.205
  10.1 0.4 fusion.7
  10.5 1.1 copy.25
  11.6 0.7 all-gather.5.cloned.1.call-update
  12.5 0.4 reshape.207
  12.9 0.6 fusion.25
  14.8 14.3 %all-reduce.2 = bf16[2240]{0:T(1024)(128)(2,1)S(1)} all-reduce(bf16[2240]{0:T(1024)(128)(2,1)S(1)} %get-tuple-element.8), channel_id=3, replica_groups=mesh['groups'=2,'frame'=4,'row'=4] {'row'}, use_global_device_ids=true, to_apply=%region_3.0.clone | all-reduce | flops 2240 | bytes 8960
  29.3 7.2 %reduce-scatter.3.cloned.1.call-done = bf16[112,560]{0,1:T(8,128)(2,1)} async-done(((bf16[112,2240]{0,1:T(8,128)(2,1)}), bf16[112,560]{0,1:T(8,128)(2,1)}) %reduce-scatter.3.cloned.1.call-update) | async-done | bytes 125456 | tf_op jit(solution)/shard_map/reduce_scatter | solution.py:59
  36.5 13.6 %all-reduce.5 = (f32[112,560]{0,1:T(8,128)S(1)}, f32[560]{0:T(1024)S(1)}) all-reduce(bf16[112,560]{0,1:T(8,128)(2,1)} %reduce-scatter.3.cloned.1.call-done, f32[560]{0:T(1024)S(1)} %dynamic-slice_convert_fusion), channel_id=1, replica_groups=mesh['groups'=2,'frame'=4,'row'=4] {'frame'}, use_global_device_ids=true, to_apply=%region_1.0 | all-reduce | flops 63280 | bytes 380800 | tf_op jit(solution)/shard_map/psum | solution.py:66
  50.1 0.3 dynamic-update-slice
  50.4 19.7 %all-reduce.1 = f32[2240]{0:T(1024)S(1)} all-reduce(f32[2240]{0:T(1024)S(1)} %dynamic-update-slice), channel_id=1, replica_groups=mesh['groups'=2,'frame'=4,'row'=4] {'row'}, use_global_device_ids=true, to_apply=%add.1 | all-reduce | flops 2240 | bytes 17920
  70.2 0.6 fusion.17
  70.8 42.0 %all_gather.12 = f32[112,2240]{0,1:T(8,128)S(1)} all-gather(f32[112,560]{0,1:T(8,128)S(1)} %get-tuple-element.2), channel_id=1, replica_groups=mesh['groups'=2,'frame'=4,'row'=4] {'row'}, dimensions={1}, use_global_device_ids=true | all-gather | bytes 1254400 | tf_op jit(solution)/shard_map/all_gather | solution.py:68
  112.8 1.4 multiply_reduce_fusion
  114.2 0.4 copy.28
  115.4 1.0 multiply_convert_fusion.1
  116.6 82.5 %all-gather.5.cloned.1.call-done = bf16[2240,2,840]{2,1,0:T(2,128)(2,1)} async-done(((bf16[560,2,840]{2,1,0:T(2,128)(2,1)}), bf16[2240,2,840]{2,1,0:T(2,128)(2,1)}) %all-gather.5.cloned.1.call-update) | async-done | bytes 7526416 | tf_op jit(solution)/shard_map/all_gather | solution.py:87
  199.1 22.9 %copy.30 = bf16[2240,2,840]{0,2,1:T(8,128)(2,1)} copy(bf16[2240,2,840]{2,1,0:T(2,128)(2,1)} %all-gather.5.cloned.1.call-done) | data formatting | bytes 15052800 | tf_op jit(solution)/shard_map/all_gather | solution.py:87
  221.9 5.8 %multiply_convert_fusion = bf16[256,1680]{0,1:T(8,128)(2,1)S(1)} fusion(bf16[256,2240]{1,0:T(8,128)(2,1)} %bitcast.49, bf16[2240,1680]{0,1:T(8,128)(2,1)} %bitcast.45), kind=kOutput, calls=%fused_computation.10 | convolution fusion | flops 1928908800 | bytes 9533440 | tf_op jit(solution)/shard_map/dot_general | solution.py:94
  227.8 0.6 copy.31
  228.4 1.3 collective-permute-start.1
  229.7 4.8 %collective-permute-start = (bf16[4,1,64,1680]{3,2,0,1:T(8,128)(2,1)S(1)}, bf16[4,1,64,1680]{3,2,0,1:T(8,128)(2,1)S(1)}, u32[]{:S(2)}, u32[]{:S(2)}) collective-permute-start(bf16[4,1,64,1680]{3,2,0,1:T(8,128)(2,1)S(1)} %bitcast.42), channel_id=1, source_target_pairs={{0,1},{1,2},{2,3},{4,5},{5,6},{6,7},{8,9},{9,10},{10,11},{12,13},{... | collective-permute-start | bytes 2580488 | tf_op jit(solution)/shard_map/ppermute | solution.py:20
  235.2 17.3 %collective-permute-done.1 = bf16[4,1,64,1680]{3,2,0,1:T(8,128)(2,1)S(1)} collective-permute-done((bf16[4,1,64,1680]{3,2,0,1:T(8,128)(2,1)S(1)}, bf16[4,1,64,1680]{3,2,0,1:T(8,128)(2,1)S(1)}, u32[]{:S(2)}, u32[]{:S(2)}) %collective-permute-start.1) | collective-permute-done | bytes 860192 | tf_op jit(solution)/shard_map/ppermute | solution.py:22
  252.6 1.2 collective-permute-done
  253.8 1.1 fusion.5
  254.9 1.8 multiply_add_fusion
  256.6 0.3 fusion.8
  257.0 2.4 convolution_convert_fusion
  259.4 26.0 %reduce-scatter.5.cloned.1.call-done = bf16[64,2240]{1,0:T(8,128)(2,1)} async-done(((bf16[256,2240]{1,0:T(8,128)(2,1)}), bf16[64,2240]{1,0:T(8,128)(2,1)}) %reduce-scatter.5.cloned.1.call-update) | async-done | bytes 286736 | tf_op jit(solution)/shard_map/reduce_scatter | solution.py:107
  285.4 1.7 fusion.16
  (44 shorter events, 2.0 us)
Async XLA Ops:
  7.2 29.3 %reduce-scatter.3.cloned.1.call-start = ((), (), s32[]{:S(2)}) async-start(), calls=%async_computation.2 | async-start | bytes 716800 | tf_op jit(solution)/shard_map/reduce_scatter | solution.py:59
  10.4 2.0 copy-start.3
  10.5 2.0 copy-start.4
  10.5 2.0 copy-start.1
  11.6 1.4 copy-start.5
  11.6 187.5 %all-gather.5.cloned.1.call-start = ((), (), s32[]{:S(2)}) async-start(), calls=%async_computation.4 | async-start | bytes 10035200 | tf_op jit(solution)/shard_map/all_gather | solution.py:87
  12.4 209.6 %all-gather.3.cloned.1.call-start = ((), (), s32[]{:S(2)}) async-start(), calls=%async_computation.3 | async-start | bytes 1474560 | tf_op jit(solution)/shard_map/all_gather | solution.py:91
  114.2 1.0 copy-start
  116.5 168.9 %reduce-scatter.5.cloned.1.call-start = ((), (), s32[]{:S(2)}) async-start(), calls=%async_computation.5 | async-start | bytes 1474560 | tf_op jit(solution)/shard_map/reduce_scatter | solution.py:107
  221.9 12.6 %copy-start.2 = (bf16[9,2,840]{2,1,0:T(2,128)(2,1)S(1)}, bf16[9,2,840]{2,1,0:T(2,128)(2,1)}, u32[]{:S(2)}) copy-start(bf16[9,2,840]{2,1,0:T(2,128)(2,1)} %param.16) | copy-start | bytes 90724
  228.4 24.2 %collective-permute-start.1 = (bf16[4,1,64,1680]{3,2,0,1:T(8,128)(2,1)S(1)}, bf16[4,1,64,1680]{3,2,0,1:T(8,128)(2,1)S(1)}, u32[]{:S(2)}, u32[]{:S(2)}) collective-permute-start(bf16[4,1,64,1680]{3,2,0,1:T(8,128)(2,1)S(1)} %bitcast.41), channel_id=1, source_target_pairs={{1,0},{2,1},{3,2},{5,4},{6,5},{7,6},{9,8},{10,9},{11,10},{13,12},{... | collective-permute-start | bytes 2580488 | tf_op jit(solution)/shard_map/ppermute | solution.py:22
  229.7 24.1 %collective-permute-start = (bf16[4,1,64,1680]{3,2,0,1:T(8,128)(2,1)S(1)}, bf16[4,1,64,1680]{3,2,0,1:T(8,128)(2,1)S(1)}, u32[]{:S(2)}, u32[]{:S(2)}) collective-permute-start(bf16[4,1,64,1680]{3,2,0,1:T(8,128)(2,1)S(1)} %bitcast.42), channel_id=1, source_target_pairs={{0,1},{1,2},{2,3},{4,5},{5,6},{6,7},{8,9},{9,10},{10,11},{12,13},{... | collective-permute-start | bytes 2580488 | tf_op jit(solution)/shard_map/ppermute | solution.py:20
  254.8 2.1 copy-start.6
Sparse Core Ops, SparseCore 0:
  11.7 24.6 reduce-scatter.2
  38.0 160.9 all-gather.4
  201.2 15.6 all-gather.2
  259.5 25.7 reduce-scatter.4
where the time goes:
time: 295 us; the launch traced here: 294 us
  waiting for transfers between devices  135 us (46%)
  blocking collectives  89.6 us (30%)
  local copies, waits for them, and re-layouts  29.5 us (10%)
  between operations  15.4 us (5%)
  matrix products  10.6 us (4%)
  other arithmetic  7.42 us (3%)
  starting transfers between devices  6.24 us (2%)
    all_gather x1, waiting for transfers between devices, local(): lax.all_gather(in_weight, 'row', axis=0, tiled=True)  82.5 us
    all_gather x1, blocking collectives, local(): lax.all_gather(state_share, 'row', axis=1, tiled=True)  42 us
    unnamed x2, blocking collectives  34 us
    reduce_scatter x1, waiting for transfers between devices, local(): lax.psum_scatter(jnp.dot(hidden_flat, out_weight, preferred_element_type=...  26 us
    all_gather x1, local copies, waits for them, and re-layouts, local(): lax.all_gather(in_weight, 'row', axis=0, tiled=True)  22.9 us
    ppermute x1, waiting for transfers between devices, padded_2(): lax.ppermute(head, axis, [((i + 1) % count, i) for i in range(ends)])  17.3 us
    psum x1, blocking collectives, local(): state_share, total_share = lax.psum((state_share, total_share), 'frame')  13.6 us
    reduce_scatter x1, waiting for transfers between devices, local(): lax.psum_scatter(local_state.astype(jnp.bfloat16), 'row', scatter_dimensi...  7.19 us
  transfers between devices with their start and end apart: 6, of which 5 were waited for; matrix products, arithmetic and copies ran while one was open for 10% of the time, Pallas kernels for 0%

commit v1 on v0

--- a/solution.py
+++ b/solution.py
@@ -7,6 +7,24 @@
 HEAD_DIM = 112
 NORM_EPS = 1e-06
 SHARE_EPS = 1e-06
+
+
+def ring_gather(value, axis, dim):
+    ways, here, step = (lax.axis_size(axis), lax.axis_index(axis), value.shape[dim])
+    shape = [n * ways if d == dim else n for d, n in enumerate(value.shape)]
+    full = lax.dynamic_update_slice_in_dim(
+        jnp.zeros(shape, value.dtype), value, here * step, axis=dim
+    )
+    going_up = going_down = value
+    for far in range(1, ways // 2 + 1):
+        going_up = lax.ppermute(going_up, axis, [(d, (d + 1) % ways) for d in range(ways)])
+        full = lax.dynamic_update_slice_in_dim(full, going_up, (here - far) % ways * step, axis=dim)
+        if 2 * far < ways:
+            going_down = lax.ppermute(going_down, axis, [(d, (d - 1) % ways) for d in range(ways)])
+            full = lax.dynamic_update_slice_in_dim(
+                full, going_down, (here + far) % ways * step, axis=dim
+            )
+    return full
 
 
 def padded_2(cells, sides, width):
@@ -84,9 +102,7 @@
         jnp.bfloat16
     )
     normed_grid = normed.reshape(frame_count, row_count, col_count, model_width)
-    in_full = lax.all_gather(in_weight, "row", axis=0, tiled=True).reshape(
-        model_width, 2 * local_gated
-    )
+    in_full = ring_gather(in_weight, "row", 0).reshape(model_width, 2 * local_gated)
     conv_taps = conv_weight.reshape(9, 2 * local_gated).astype(jnp.float32)
     frame_piece = lax.all_gather(normed_grid, "frame", axis=0, tiled=True)
     piece_frames = frame_piece.shape[0]

time: 295 us -> 355 us (1.20)
  waiting for transfers between devices: 135 us -> 41.9 us
  local copies, waits for them, and re-layouts: 29.5 us -> 118 us
  blocking collectives: 89.6 us -> 148 us
  starting transfers between devices: 6.24 us -> 10.2 us
    dynamic_update_slice x0 -> x4, local copies, waits for them, and re-layouts: none -> 90.5 us  [the longest x2 45.9 us: ring_gather(): lax.dynamic_update_slice_in_dim(full, going_up, (here - far) % ways * ste...]
    all_gather x1 -> x0, waiting for transfers between devices: 82.5 us -> none  [local(): lax.all_gather(in_weight, 'row', axis=0, tiled=True)]
    unnamed x2, blocking collectives: 34 us -> 113 us
    all_gather x1 -> x0, local copies, waits for them, and re-layouts: 22.9 us -> none  [local(): lax.all_gather(in_weight, 'row', axis=0, tiled=True)]
    all_gather x1, blocking collectives: 42 us -> 20.6 us  [local(): lax.all_gather(state_share, 'row', axis=1, tiled=True)]
    ppermute x1, waiting for transfers between devices: 17.3 us -> 5.5 us  [padded_2(): lax.ppermute(head, axis, [((i + 1) % count, i) for i in range(ends)])]
    ppermute x1, waiting for transfers between devices: 1.18 us -> 12.1 us  [padded_2(): lax.ppermute(tail, axis, [(i, (i + 1) % count) for i in range(ends)])]
    ppermute x0 -> x3, local copies, waits for them, and re-layouts: none -> 10.6 us  [the longest x2 7.09 us: ring_gather(): lax.ppermute(going_up, axis, [(d, (d + 1) % ways) for d in range(ways)])]
  transfers between devices with their start and end apart: 6 -> 8, of which waited for: 5 -> 3; matrix products, arithmetic and copies ran while one was open for 10% -> 33% of each run, Pallas kernels for 0% -> 0%
where the time goes in v1:
time: 355 us; the launch traced here: 351 us
  blocking collectives  148 us (42%)
  local copies, waits for them, and re-layouts  118 us (33%)
  waiting for transfers between devices  41.9 us (12%)
  between operations  15.4 us (4%)
  matrix products  10.6 us (3%)
  starting transfers between devices  10.2 us (3%)
  other arithmetic  7.45 us (2%)
    unnamed x2, blocking collectives  113 us
    dynamic_update_slice x2, local copies, waits for them, and re-layouts, ring_gather(): lax.dynamic_update_slice_in_dim(full, going_up, (here - far) % ways * ste...  45.9 us
    reduce_scatter x1, waiting for transfers between devices, local(): lax.psum_scatter(jnp.dot(hidden_flat, out_weight, preferred_element_type=...  24.3 us
    dynamic_update_slice x1, local copies, waits for them, and re-layouts, ring_gather(): lax.dynamic_update_slice_in_dim(full, going_down, (here + far) % ways * s...  23.5 us
    dynamic_update_slice x1, local copies, waits for them, and re-layouts, ring_gather(): lax.dynamic_update_slice_in_dim(jnp.zeros(shape, value.dtype), value, her...  21.1 us
    all_gather x1, blocking collectives, local(): lax.all_gather(state_share, 'row', axis=1, tiled=True)  20.6 us
    psum x1, blocking collectives, local(): state_share, total_share = lax.psum((state_share, total_share), 'frame')  13.8 us
    ppermute x1, waiting for transfers between devices, padded_2(): lax.ppermute(tail, axis, [(i, (i + 1) % count) for i in range(ends)])  12.1 us
  transfers between devices with their start and end apart: 8, of which 3 were waited for; matrix products, arithmetic and copies ran while one was open for 33% of the time, Pallas kernels for 0%

profile of v1, /device:TPU:0, one launch (start us, length us, event | category | flops | bytes accessed | tf_op | source)
XLA Modules:
  0.0 351.5 jit_solution(9925255957794126768)
XLA Ops:
  7.2 1.1 fusion.21
  8.7 1.5 reshape.205
  10.6 1.1 copy.27
  11.8 1.5 copy.33
  13.4 3.0 collective-permute-start
  16.4 2.0 collective-permute-start.1
  20.8 97.5 %all-reduce.2 = bf16[2240]{0:T(1024)(128)(2,1)S(1)} all-reduce(bf16[2240]{0:T(1024)(128)(2,1)S(1)} %get-tuple-element.8), channel_id=3, replica_groups=mesh['groups'=2,'frame'=4,'row'=4] {'row'}, use_global_device_ids=true, to_apply=%region_3.0.clone | all-reduce | flops 2240 | bytes 8960
  118.5 13.8 %all-reduce.5 = (f32[112,560]{0,1:T(8,128)S(1)}, f32[560]{0:T(1024)S(1)}) all-reduce(bf16[112,560]{0,1:T(8,128)(2,1)} %reduce-scatter.3.cloned.1.call-done, f32[560]{0:T(1024)S(1)} %dynamic-slice_convert_fusion), channel_id=1, replica_groups=mesh['groups'=2,'frame'=4,'row'=4] {'frame'}, use_global_device_ids=true, to_apply=%region_1.0 | all-reduce | flops 63280 | bytes 380800 | tf_op jit(solution)/shard_map/psum | solution.py:84
  132.6 15.8 %all-reduce.1 = f32[2240]{0:T(1024)S(1)} all-reduce(f32[2240]{0:T(1024)S(1)} %dynamic-update-slice), channel_id=1, replica_groups=mesh['groups'=2,'frame'=4,'row'=4] {'row'}, use_global_device_ids=true, to_apply=%add.1 | all-reduce | flops 2240 | bytes 17920
  148.5 0.6 fusion.17
  149.1 20.6 %all_gather.9 = f32[112,2240]{0,1:T(8,128)S(1)} all-gather(f32[112,560]{0,1:T(8,128)S(1)} %get-tuple-element.2), channel_id=1, replica_groups=mesh['groups'=2,'frame'=4,'row'=4] {'row'}, dimensions={1}, use_global_device_ids=true | all-gather | bytes 1254400 | tf_op jit(solution)/shard_map/all_gather | solution.py:86
  169.7 1.4 multiply_reduce_fusion
  172.6 1.0 multiply_convert_fusion.1
  173.9 5.0 %copy.32 = bf16[560,2,840]{0,2,1:T(8,128)(2,1)S(1)} copy(bf16[560,2,840]{2,1,0:T(2,128)(2,1)} %param.15) | data formatting | bytes 3763200 | tf_op args[6]
  178.9 3.7 %broadcast_in_dim.2 = bf16[2240,2,840]{0,2,1:T(8,128)(2,1)} broadcast(bf16[]{:T(256)} %constant.42.clone.1), dimensions={} | broadcast | bytes 7526402 | tf_op jit(solution)/shard_map/broadcast_in_dim | solution.py:16
  182.5 21.1 %dynamic_update_slice.12 = bf16[2240,2,840]{0,2,1:T(8,128)(2,1)} dynamic-update-slice(bf16[2240,2,840]{0,2,1:T(8,128)(2,1)} %broadcast_in_dim.2, bf16[560,2,840]{0,2,1:T(8,128)(2,1)S(1)} %copy.32, s32[]{:T(128)S(6)} %select_n.27, s32[]{:T(128)} %constant.48.clone.1, s32[]{:T(128)} %constant.48.clone.1) | dynamic-update-slice | bytes 3763204 | tf_op jit(solution)/shard_map/dynamic_update_slice | solution.py:15
  203.7 3.5 %copy.34 = bf16[560,2,840]{0,2,1:T(8,128)(2,1)S(1)} copy(bf16[560,2,840]{2,0,1:T(8,128)(2,1)} %collective-permute-done) | data formatting | bytes 3763200 | tf_op jit(solution)/shard_map/ppermute | solution.py:20
  207.2 22.4 %dynamic_update_slice.13 = bf16[2240,2,840]{0,2,1:T(8,128)(2,1)} dynamic-update-slice(bf16[2240,2,840]{0,2,1:T(8,128)(2,1)} %dynamic_update_slice.12, bf16[560,2,840]{0,2,1:T(8,128)(2,1)S(1)} %copy.34, s32[]{:T(128)S(6)} %select_n.29, s32[]{:T(128)} %constant.48.clone.1, s32[]{:T(128)} %constant.48.clone.1) | dynamic-update-slice | bytes 3763204 | tf_op jit(solution)/shard_map/dynamic_update_slice | solution.py:21
  229.6 3.5 %copy.36 = bf16[560,2,840]{0,2,1:T(8,128)(2,1)S(1)} copy(bf16[560,2,840]{2,0,1:T(8,128)(2,1)} %collective-permute-done.1) | data formatting | bytes 3763200 | tf_op jit(solution)/shard_map/ppermute | solution.py:23
  233.2 23.5 %dynamic_update_slice.14 = bf16[2240,2,840]{0,2,1:T(8,128)(2,1)} dynamic-update-slice(bf16[2240,2,840]{0,2,1:T(8,128)(2,1)} %dynamic_update_slice.13, bf16[560,2,840]{0,2,1:T(8,128)(2,1)S(1)} %copy.36, s32[]{:T(128)S(6)} %select_n.31, s32[]{:T(128)} %constant.48.clone.1, s32[]{:T(128)} %constant.48.clone.1) | dynamic-update-slice | bytes 3763204 | tf_op jit(solution)/shard_map/dynamic_update_slice | solution.py:24
  256.7 3.5 %copy.37 = bf16[560,2,840]{0,2,1:T(8,128)(2,1)S(1)} copy(bf16[560,2,840]{2,0,1:T(8,128)(2,1)} %collective-permute-done.2) | data formatting | bytes 3763200 | tf_op jit(solution)/shard_map/ppermute | solution.py:20
  260.2 23.5 %dynamic_update_slice.15 = bf16[2240,2,840]{0,2,1:T(8,128)(2,1)} dynamic-update-slice(bf16[2240,2,840]{0,2,1:T(8,128)(2,1)} %dynamic_update_slice.14, bf16[560,2,840]{0,2,1:T(8,128)(2,1)S(1)} %copy.37, s32[]{:T(128)S(6)} %select_n.33, s32[]{:T(128)} %constant.48.clone.1, s32[]{:T(128)} %constant.48.clone.1) | dynamic-update-slice | bytes 3763204 | tf_op jit(solution)/shard_map/dynamic_update_slice | solution.py:21
  283.7 5.8 %multiply_convert_fusion = bf16[256,1680]{0,1:T(8,128)(2,1)S(1)} fusion(bf16[256,2240]{1,0:T(8,128)(2,1)} %bitcast.49, bf16[2240,1680]{0,1:T(8,128)(2,1)} %bitcast.45), kind=kOutput, calls=%fused_computation.10 | convolution fusion | flops 1928908800 | bytes 9533440 | tf_op jit(solution)/shard_map/dot_general | solution.py:110
  290.2 3.4 collective-permute-start.3
  293.6 1.3 collective-permute-start.4
  295.7 12.1 %collective-permute-done.3 = bf16[4,1,64,1680]{3,2,0,1:T(8,128)(2,1)S(1)} collective-permute-done((bf16[4,1,64,1680]{3,2,0,1:T(8,128)(2,1)S(1)}, bf16[4,1,64,1680]{3,2,0,1:T(8,128)(2,1)S(1)}, u32[]{:S(2)}, u32[]{:S(2)}) %collective-permute-start.3) | collective-permute-done | bytes 860192 | tf_op jit(solution)/shard_map/ppermute | solution.py:38
  307.7 5.5 %collective-permute-done.4 = bf16[4,1,64,1680]{3,2,0,1:T(8,128)(2,1)S(1)} collective-permute-done((bf16[4,1,64,1680]{3,2,0,1:T(8,128)(2,1)S(1)}, bf16[4,1,64,1680]{3,2,0,1:T(8,128)(2,1)S(1)}, u32[]{:S(2)}, u32[]{:S(2)}) %collective-permute-start.4) | collective-permute-done | bytes 860192 | tf_op jit(solution)/shard_map/ppermute | solution.py:40
  313.2 1.1 fusion.5
  314.3 1.8 multiply_add_fusion
  316.5 2.4 convolution_convert_fusion
  318.9 24.3 %reduce-scatter.5.cloned.1.call-done = bf16[64,2240]{1,0:T(8,128)(2,1)} async-done(((bf16[256,2240]{1,0:T(8,128)(2,1)}), bf16[64,2240]{1,0:T(8,128)(2,1)}) %reduce-scatter.5.cloned.1.call-update) | async-done | bytes 286736 | tf_op jit(solution)/shard_map/reduce_scatter | solution.py:123
  343.2 1.7 fusion.16
  (58 shorter events, 5.8 us)
Async XLA Ops:
  7.2 111.3 %reduce-scatter.3.cloned.1.call-start = ((), (), s32[]{:S(2)}) async-start(), calls=%async_computation.2 | async-start | bytes 716800 | tf_op jit(solution)/shard_map/reduce_scatter | solution.py:77
  8.7 3.1 copy-start
  11.7 6.7 %copy-start.2 = (bf16[1,1,64,2240]{3,2,1,0:T(8,128)(2,1)S(1)}, bf16[1,1,64,2240]{3,2,1,0:T(8,128)(2,1)}, u32[]{:S(2)}) copy-start(bf16[1,1,64,2240]{3,2,1,0:T(8,128)(2,1)} %param.9) | copy-start | bytes 860164
  11.7 7.1 %copy-start.4 = (bf16[2240]{0:T(1024)(128)(2,1)S(1)}, bf16[2240]{0:T(1024)(128)(2,1)}, u32[]{:S(2)}) copy-start(bf16[2240]{0:T(1024)(128)(2,1)} %param.13) | copy-start | bytes 13444
  11.7 7.2 %copy-start.5 = (bf16[2240]{0:T(1024)(128)(2,1)S(1)}, bf16[2240]{0:T(1024)(128)(2,1)}, u32[]{:S(2)}) copy-start(bf16[2240]{0:T(1024)(128)(2,1)} %param.14) | copy-start | bytes 13444
  11.8 7.2 %copy-start.6 = (u32[32]{0:T(128)S(1)}, u32[32]{0:T(128)}, u32[]{:S(2)}) copy-start(u32[32]{0:T(128)} %constant.64) | copy-start | bytes 388
  11.8 271.9 %all-gather.2.cloned.1.call-start = ((), (), s32[]{:S(2)}) async-start(), calls=%async_computation.3 | async-start | bytes 1474560 | tf_op jit(solution)/shard_map/all_gather | solution.py:107
  13.4 159.0 %collective-permute-start = (bf16[560,2,840]{2,0,1:T(8,128)(2,1)}, bf16[560,2,840]{2,0,1:T(8,128)(2,1)}, u32[]{:S(2)}, u32[]{:S(2)}) collective-permute-start(bf16[560,2,840]{2,0,1:T(8,128)(2,1)} %copy.33), channel_id=1, source_target_pairs={{0,1},{1,2},{2,3},{3,0},{4,5},{5,6},{6,7},{7,4},{8,9},{9,10},{10,1... | collective-permute-start | bytes 5644808 | tf_op jit(solution)/shard_map/ppermute | solution.py:20
  16.4 213.2 %collective-permute-start.1 = (bf16[560,2,840]{2,0,1:T(8,128)(2,1)}, bf16[560,2,840]{2,0,1:T(8,128)(2,1)}, u32[]{:S(2)}, u32[]{:S(2)}) collective-permute-start(bf16[560,2,840]{2,0,1:T(8,128)(2,1)} %copy.33), channel_id=1, source_target_pairs={{0,3},{1,0},{2,1},{3,2},{4,7},{5,4},{6,5},{7,6},{8,11},{9,8},{10,9... | collective-permute-start | bytes 5644808 | tf_op jit(solution)/shard_map/ppermute | solution.py:23
  171.1 1.0 copy-start.1
  172.4 84.3 %collective-permute-start.2 = (bf16[560,2,840]{2,0,1:T(8,128)(2,1)}, bf16[560,2,840]{2,0,1:T(8,128)(2,1)}, u32[]{:S(2)}, u32[]{:S(2)}) collective-permute-start(bf16[560,2,840]{2,0,1:T(8,128)(2,1)} %collective-permute-done), channel_id=1, source_target_pairs={{0,1},{1,2},{2,3},{3,0},{4,5},{5,6},{6,7},{7,4},{8,9},{9,10},{10,1... | collective-permute-start | bytes 5644808 | tf_op jit(solution)/shard_map/ppermute | solution.py:20
  173.6 169.6 %reduce-scatter.5.cloned.1.call-start = ((), (), s32[]{:S(2)}) async-start(), calls=%async_computation.4 | async-start | bytes 1474560 | tf_op jit(solution)/shard_map/reduce_scatter | solution.py:123
  283.7 11.2 %copy-start.3 = (bf16[9,2,840]{2,1,0:T(2,128)(2,1)S(1)}, bf16[9,2,840]{2,1,0:T(2,128)(2,1)}, u32[]{:S(2)}) copy-start(bf16[9,2,840]{2,1,0:T(2,128)(2,1)} %param.16) | copy-start | bytes 90724
  290.2 17.6 %collective-permute-start.3 = (bf16[4,1,64,1680]{3,2,0,1:T(8,128)(2,1)S(1)}, bf16[4,1,64,1680]{3,2,0,1:T(8,128)(2,1)S(1)}, u32[]{:S(2)}, u32[]{:S(2)}) collective-permute-start(bf16[4,1,64,1680]{3,2,0,1:T(8,128)(2,1)S(1)} %bitcast.41), channel_id=1, source_target_pairs={{0,1},{1,2},{2,3},{4,5},{5,6},{6,7},{8,9},{9,10},{10,11},{12,13},{... | collective-permute-start | bytes 2580488 | tf_op jit(solution)/shard_map/ppermute | solution.py:38
  293.6 19.6 %collective-permute-start.4 = (bf16[4,1,64,1680]{3,2,0,1:T(8,128)(2,1)S(1)}, bf16[4,1,64,1680]{3,2,0,1:T(8,128)(2,1)S(1)}, u32[]{:S(2)}, u32[]{:S(2)}) collective-permute-start(bf16[4,1,64,1680]{3,2,0,1:T(8,128)(2,1)S(1)} %bitcast.42), channel_id=1, source_target_pairs={{1,0},{2,1},{3,2},{5,4},{6,5},{7,6},{9,8},{10,9},{11,10},{13,12},{... | collective-permute-start | bytes 2580488 | tf_op jit(solution)/shard_map/ppermute | solution.py:40
  314.3 2.2 copy-start.7
Sparse Core Ops, SparseCore 0:
  11.8 65.7 reduce-scatter.2
  173.7 18.8 all-gather.1
  319.0 24.1 reduce-scatter.4
